TPU v7x, 256 devices: a whole 4x4x8 slice. The times are simulated.
256 devices in a mesh: dp: 8 (over y, x_hi), shard: 32 (over x_lo, z, core).
Axes of the slice: x: 4 (x_hi: 2, x_lo: 2; x = x_hi * 2 + x_lo), y: 4, z: 8, core: 2. Of those that a mesh axis runs over, the one named last changes fastest.
Arguments:
- grads: float32 [8, 1, 2, 4096, 4096], P('dp', None, None, None, 'shard'), may hold values from -6 to 6
- params: float32 [1, 2, 4096, 4096], P(None, None, ('dp', 'shard')), may hold values from -0.09375 to 0.09375
- moment_one: float32 [1, 2, 4096, 4096], P(None, None, ('dp', 'shard')), may hold values from -0.75 to 0.75
- moment_two: float32 [1, 2, 4096, 4096], P(None, None, ('dp', 'shard')), may hold values from 1e-05 to 0.01
- relation_ids: int32 [1], replicated, may hold values from 0 to 63
- rates: float32 [64], replicated, may hold values from 0.02 to 0.1
- step_count: int32 [1], replicated, may hold values from 1 to 8
Outputs:
- new_params: float32 [1, 2, 4096, 4096], P(None, None, ('dp', 'shard'))
- new_moment_one: float32 [1, 2, 4096, 4096], P(None, None, ('dp', 'shard'))
- new_moment_two: float32 [1, 2, 4096, 4096], P(None, None, ('dp', 'shard'))
- panels: bfloat16 [1, 2, 4096, 4096], P(None, None, None, 'shard')
Inputs may be any that keep to these rules, and one draw needn't show every extreme that they name: `relation_ids`: relation ids are edge types. `step_count`: the step count is positive.
All inputs are finite; a program needn't handle non-finite values.
Results may differ from a plain program's by a relative error of at most 0.001.
Values may be sent and summed in bfloat16 or wider, within the bound.
No kernel may reach another device: no remote copies, remote signals or barrier semaphores. Data moves between devices by JAX's collectives and lax.ppermute only.
A program may use at most 128 MiB of HBM per device.

v0:
```python
import jax
import jax.numpy as jnp
from jax import lax
from jax.sharding import PartitionSpec as P


def body(grads, params, moment_one, moment_two, relation_ids, rates, step_count):
    groups = lax.axis_size("dp")
    owners = lax.axis_size("shard")
    relations = grads.shape[1]
    rows = grads.shape[3]
    panel_cols = grads.shape[-1]
    width = panel_cols * owners
    owned = params.shape[2]
    block = rows // groups
    summed = lax.psum_scatter(grads[0], "dp", scatter_dimension=2, tiled=True)
    pieces = summed.reshape(relations, 2, owners, owned, panel_cols)
    moved = lax.all_to_all(pieces, "shard", split_axis=2, concat_axis=2, tiled=True)
    gradient = moved.transpose(0, 1, 3, 2, 4).reshape(relations, 2, owned, width) / groups
    onehot = (relation_ids[:, None] == jnp.arange(rates.shape[0], dtype=jnp.int32)[None, :]).astype(
        jnp.float32
    )
    learn = jnp.sum(onehot * rates[None, :], axis=1)[:, None, None, None]
    new_one = 0.9 * moment_one + 0.1 * gradient
    new_two = 0.95 * moment_two + 0.05 * gradient * gradient
    steps = step_count[0].astype(jnp.float32)
    fix_one = 1.0 - jnp.power(jnp.float32(0.9), steps)
    fix_two = 1.0 - jnp.power(jnp.float32(0.95), steps)
    update = new_one / fix_one / (jnp.sqrt(new_two / fix_two) + 1e-08) + 0.1 * params
    new_params = params - learn * update
    fresh = new_params.astype(jnp.bfloat16).reshape(relations, 2, owned, owners, panel_cols)
    fresh = fresh.transpose(0, 1, 3, 2, 4)
    back = lax.all_to_all(fresh, "shard", split_axis=2, concat_axis=2, tiled=True)
    back = back.reshape(relations, 2, block, panel_cols)
    panels = lax.all_gather(back, "dp", axis=2, tiled=True)
    return (new_params, new_one, new_two, panels)


def solution(mesh):
    in_specs = (
        P("dp", None, None, None, "shard"),
        P(None, None, ("dp", "shard"), None),
        P(None, None, ("dp", "shard"), None),
        P(None, None, ("dp", "shard"), None),
        P(),
        P(),
        P(),
    )
    out_specs = (
        P(None, None, ("dp", "shard"), None),
        P(None, None, ("dp", "shard"), None),
        P(None, None, ("dp", "shard"), None),
        P(None, None, None, "shard"),
    )
    return jax.shard_map(body, mesh=mesh, in_specs=in_specs, out_specs=out_specs, check_vma=False)
```

profile of v0, /device:TPU:1, one launch (start us, length us, event | category | flops | bytes accessed | tf_op | source)
XLA Modules:
  0.0 216.3 jit_solution(13947312932788557129)
XLA Ops:
  7.2 0.0 reduce-scatter.2.cloned.1.call-start
  7.2 0.7 reduce-scatter.2.cloned.1.call-update
  7.9 0.0 copy-start.3
  7.9 0.0 copy-start
  7.9 0.0 copy-start.1
  7.9 0.0 copy-start.2
  7.9 96.5 %reduce-scatter.2.cloned.1.call-done = f32[1,2,512,128]{3,2,1,0:T(8,128)} async-done(((f32[1,2,4096,128]{3,2,1,0:T(8,128)}), f32[1,2,512,128]{3,2,1,0:T(8,128)}) %reduce-scatter.2.cloned.1.call-update) | async-done | bytes 524304 | tf_op jit(solution)/shard_map/reduce_scatter | solution.py:16
  104.5 1.9 copy.29
  106.4 9.3 %all-to-all-start = ((f32[1,2,32,16,128]{4,3,1,0,2:T(8,128)}), f32[1,2,32,16,128]{4,3,1,0,2:T(8,128)S(1)}, u32[]{:S(2)}, u32[]{:S(2)}) async-start(f32[1,2,32,16,128]{4,3,1,0,2:T(8,128)} %copy.29), calls=%async_computation.1 | async-start | bytes 1048576 | tf_op jit(solution)/shard_map/all_to_all | solution.py:18
  115.7 0.0 all-gather.2.cloned.1.call-start
  117.1 0.0 copy-done.3
  117.1 0.7 fusion
  117.8 14.5 %all-to-all-done = f32[1,2,32,16,128]{4,3,1,0,2:T(8,128)S(1)} async-done(((f32[1,2,32,16,128]{4,3,1,0,2:T(8,128)}), f32[1,2,32,16,128]{4,3,1,0,2:T(8,128)S(1)}, u32[]{:S(2)}, u32[]{:S(2)}) %all-to-all-start) | async-done | bytes 524320 | tf_op jit(solution)/shard_map/all_to_all | solution.py:18
  132.3 0.4 copy_multiply_fusion
  132.6 0.0 copy-done
  132.6 0.0 copy-done.1
  132.7 0.0 copy-done.2
  132.7 2.5 %fusion.1 = (bf16[1,2,16,4096]{3,2,1,0:T(8,128)(2,1)S(1)}, f32[1,2,16,4096]{3,2,1,0:T(8,128)}, f32[1,2,16,4096]{3,2,1,0:T(8,128)}, f32[1,2,16,4096]{3,2,1,0:T(8,128)}) fusion(f32[1,2,16,4096]{3,2,1,0:T(8,128)S(1)} %copy-done, f32[]{:T(128)} %bitcast.8, f32[]{:T(128)} %bitcast.5, f32[]{:T(128)} %fusion, f32[1,2,16,4096]{3,0,2,1:T(1,128)S(1)} %bitcast.22, ...), kind=kLoop, calls=%fused_computation.7 | loop fusion | flops 1703936 | bytes 4456460 | tf_op jit(solution)/shard_map/convert_element_type | solution.py:31
  135.3 0.1 copy.35
  135.4 16.6 %all_to_all.10 = bf16[1,2,32,16,128]{4,3,1,0,2:T(8,128)(2,1)S(1)} all-to-all(bf16[1,2,32,16,128]{4,3,1,0,2:T(8,128)(2,1)S(1)} %copy.35), channel_id=1, replica_groups=mesh['dp'=8,'shard'=32] {'shard'}, dimensions={2} | all-to-all | bytes 524288 | tf_op jit(solution)/shard_map/all_to_all | solution.py:33
  152.0 0.7 copy.36
  152.7 0.0 all-gather.2.cloned.1.call-update
  152.7 53.7 %all-gather.2.cloned.1.call-done = bf16[1,2,4096,128]{3,2,1,0:T(8,128)(2,1)} async-done(((bf16[1,2,512,128]{3,2,1,0:T(8,128)(2,1)}), bf16[1,2,4096,128]{3,2,1,0:T(8,128)(2,1)}) %all-gather.2.cloned.1.call-update) | async-done | bytes 2097168 | tf_op jit(solution)/shard_map/all_gather | solution.py:35
  206.4 3.0 %copy.47 = bf16[1,2,4096,128]{3,2,1,0:T(8,128)(2,1)} copy(bf16[1,2,4096,128]{3,2,1,0:T(8,128)(2,1)} %all-gather.2.cloned.1.call-done) | data formatting | bytes 4194304
  (1 shorter events, 0.0 us)
Async XLA Ops:
  7.2 97.3 %reduce-scatter.2.cloned.1.call-start = ((), (), s32[]{:S(2)}) async-start(), calls=%async_computation.3 | async-start | bytes 4718592 | tf_op jit(solution)/shard_map/reduce_scatter | solution.py:16
  7.9 109.2 %copy-start.3 = (f32[64]{0:T(128)S(1)}, f32[64]{0:T(128)}, u32[]{:S(2)}) copy-start(f32[64]{0:T(128)} %param.12) | copy-start | bytes 772
  7.9 124.7 %copy-start = (f32[1,2,16,4096]{3,2,1,0:T(8,128)S(1)}, f32[1,2,16,4096]{3,2,1,0:T(8,128)}, u32[]{:S(2)}) copy-start(f32[1,2,16,4096]{3,2,1,0:T(8,128)} %param.8) | copy-start | bytes 1572868
  7.9 124.7 %copy-start.1 = (f32[1,2,16,4096]{3,2,1,0:T(8,128)S(1)}, f32[1,2,16,4096]{3,2,1,0:T(8,128)}, u32[]{:S(2)}) copy-start(f32[1,2,16,4096]{3,2,1,0:T(8,128)} %param.10) | copy-start | bytes 1572868
  7.9 124.7 %copy-start.2 = (f32[1,2,16,4096]{3,2,1,0:T(8,128)S(1)}, f32[1,2,16,4096]{3,2,1,0:T(8,128)}, u32[]{:S(2)}) copy-start(f32[1,2,16,4096]{3,2,1,0:T(8,128)} %param.9) | copy-start | bytes 1572868
  106.4 25.9 %all-to-all-start = ((f32[1,2,32,16,128]{4,3,1,0,2:T(8,128)}), f32[1,2,32,16,128]{4,3,1,0,2:T(8,128)S(1)}, u32[]{:S(2)}, u32[]{:S(2)}) async-start(f32[1,2,32,16,128]{4,3,1,0,2:T(8,128)} %copy.29), calls=%async_computation.1 | async-start | bytes 1048576 | tf_op jit(solution)/shard_map/all_to_all | solution.py:18
  115.7 90.8 %all-gather.2.cloned.1.call-start = ((), (), s32[]{:S(2)}) async-start(), calls=%async_computation.4 | async-start | bytes 2359296 | tf_op jit(solution)/shard_map/all_gather | solution.py:35
Sparse Core Ops, SparseCore 0:
  12.1 92.3 reduce-scatter.1
  152.8 53.5 all-gather.1
where the time goes:
time: 217 us; the launch traced here: 216 us
  waiting for transfers between devices  165 us (76%)
  blocking collectives  16.6 us (8%)
  between operations  15.5 us (7%)
  starting transfers between devices  9.35 us (4%)
  local copies, waits for them, and re-layouts  5.83 us (3%)
  other arithmetic  3.57 us (2%)
    reduce_scatter x1, waiting for transfers between devices, body(): summed = lax.psum_scatter(grads[0], 'dp', scatter_dimension=2, tiled=True)  96.5 us
    all_gather x1, waiting for transfers between devices, body(): panels = lax.all_gather(back, 'dp', axis=2, tiled=True)  53.7 us
    all_to_all x1, blocking collectives, body(): lax.all_to_all(fresh, 'shard', split_axis=2, concat_axis=2, tiled=True)  16.6 us
    all_to_all x1, waiting for transfers between devices, body(): lax.all_to_all(pieces, 'shard', split_axis=2, concat_axis=2, tiled=True)  14.5 us
    all_to_all x1, starting transfers between devices, body(): lax.all_to_all(pieces, 'shard', split_axis=2, concat_axis=2, tiled=True)  9.27 us
  transfers between devices with their start and end apart: 3, of which 3 were waited for; matrix products, arithmetic and copies ran while one was open for 0% of the time, Pallas kernels for 0%

commit v1 on v0

--- a/solution.py
+++ b/solution.py
@@ -2,6 +2,15 @@
 import jax.numpy as jnp
 from jax import lax
 from jax.sharding import PartitionSpec as P
+
+
+def part_the_files(incoming_x):
+    return jnp.concatenate(
+        lax.all_to_all(
+            jnp.stack([incoming_x] * lax.axis_size("dp")), "dp", split_axis=0, concat_axis=0
+        ),
+        axis=2,
+    )
 
 
 def body(grads, params, moment_one, moment_two, relation_ids, rates, step_count):
@@ -32,7 +41,7 @@
     fresh = fresh.transpose(0, 1, 3, 2, 4)
     back = lax.all_to_all(fresh, "shard", split_axis=2, concat_axis=2, tiled=True)
     back = back.reshape(relations, 2, block, panel_cols)
-    panels = lax.all_gather(back, "dp", axis=2, tiled=True)
+    panels = part_the_files(back)
     return (new_params, new_one, new_two, panels)
 
 

time: 217 us -> 193 us (0.89)
  waiting for transfers between devices: 165 us -> 112 us
  blocking collectives: 16.6 us -> 47.7 us
    all_gather x1 -> x0, waiting for transfers between devices: 53.7 us -> none  [body(): panels = lax.all_gather(back, 'dp', axis=2, tiled=True)]
    all_to_all x0 -> x1, blocking collectives: none -> 31.1 us  [part_the_files(): lax.all_to_all(jnp.stack([incoming_x] * lax.axis_size('dp')), 'dp', split...]
    unnamed x10 -> x9, local copies, waits for them, and re-layouts: 3.1 us -> 0.06 us
  transfers between devices with their start and end apart: 3 -> 2, of which waited for: 3 -> 2; matrix products, arithmetic and copies ran while one was open for 0% -> 0% of each run, Pallas kernels for 0% -> 0%
where the time goes in v1:
time: 193 us; the launch traced here: 192 us
  waiting for transfers between devices  112 us (58%)
  blocking collectives  47.7 us (25%)
  between operations  15.5 us (8%)
  starting transfers between devices  9.31 us (5%)
  local copies, waits for them, and re-layouts  3.95 us (2%)
  other arithmetic  3.66 us (2%)
    reduce_scatter x1, waiting for transfers between devices, body(): summed = lax.psum_scatter(grads[0], 'dp', scatter_dimension=2, tiled=True)  96.5 us
    all_to_all x1, blocking collectives, part_the_files(): lax.all_to_all(jnp.stack([incoming_x] * lax.axis_size('dp')), 'dp', split...  31.1 us
    all_to_all x1, blocking collectives, body(): lax.all_to_all(fresh, 'shard', split_axis=2, concat_axis=2, tiled=True)  16.6 us
    all_to_all x1, waiting for transfers between devices, body(): lax.all_to_all(pieces, 'shard', split_axis=2, concat_axis=2, tiled=True)  14.5 us
    all_to_all x1, starting transfers between devices, body(): lax.all_to_all(pieces, 'shard', split_axis=2, concat_axis=2, tiled=True)  9.27 us
  transfers between devices with their start and end apart: 2, of which 2 were waited for; matrix products, arithmetic and copies ran while one was open for 0% of the time, Pallas kernels for 0%

profile of v1, /device:TPU:1, one launch (start us, length us, event | category | flops | bytes accessed | tf_op | source)
XLA Modules:
  0.0 191.9 jit_solution(574999542562406544)
XLA Ops:
  7.2 0.0 reduce-scatter.2.cloned.1.call-start
  7.2 0.7 reduce-scatter.2.cloned.1.call-update
  7.9 0.0 copy-start.3
  7.9 0.0 copy-start
  7.9 0.0 copy-start.1
  7.9 0.0 copy-start.2
  7.9 96.5 %reduce-scatter.2.cloned.1.call-done = f32[1,2,512,128]{3,2,1,0:T(8,128)} async-done(((f32[1,2,4096,128]{3,2,1,0:T(8,128)}), f32[1,2,512,128]{3,2,1,0:T(8,128)}) %reduce-scatter.2.cloned.1.call-update) | async-done | bytes 524304 | tf_op jit(solution)/shard_map/reduce_scatter | solution.py:25
  104.5 1.9 copy.34
  106.4 9.3 %all-to-all-start = ((f32[1,2,32,16,128]{4,3,1,0,2:T(8,128)}), f32[1,2,32,16,128]{4,3,1,0,2:T(8,128)S(1)}, u32[]{:S(2)}, u32[]{:S(2)}) async-start(f32[1,2,32,16,128]{4,3,1,0,2:T(8,128)} %copy.34), calls=%async_computation.1 | async-start | bytes 1048576 | tf_op jit(solution)/shard_map/all_to_all | solution.py:27
  117.1 0.0 copy-done.3
  117.1 0.7 fusion
  117.7 14.5 %all-to-all-done = f32[1,2,32,16,128]{4,3,1,0,2:T(8,128)S(1)} async-done(((f32[1,2,32,16,128]{4,3,1,0,2:T(8,128)}), f32[1,2,32,16,128]{4,3,1,0,2:T(8,128)S(1)}, u32[]{:S(2)}, u32[]{:S(2)}) %all-to-all-start) | async-done | bytes 524320 | tf_op jit(solution)/shard_map/all_to_all | solution.py:27
  132.3 0.4 copy_multiply_fusion
  132.6 0.0 copy-done
  132.6 0.0 copy-done.1
  132.7 0.0 copy-done.2
  132.7 2.6 %fusion.1 = (bf16[1,2,16,4096]{3,2,1,0:T(8,128)(2,1)S(1)}, f32[1,2,16,4096]{3,2,1,0:T(8,128)}, f32[1,2,16,4096]{3,2,1,0:T(8,128)}, f32[1,2,16,4096]{3,2,1,0:T(8,128)}) fusion(f32[1,2,16,4096]{3,2,1,0:T(8,128)S(1)} %copy-done, f32[]{:T(128)} %bitcast.8, f32[]{:T(128)} %bitcast.5, f32[]{:T(128)} %fusion, f32[1,2,16,4096]{3,0,2,1:T(1,128)S(1)} %bitcast.26, ...), kind=kLoop, calls=%fused_computation.7 | loop fusion | flops 1703936 | bytes 4456460 | tf_op jit(solution)/shard_map/convert_element_type | solution.py:40
  135.3 0.1 copy.40
  135.4 16.6 %all_to_all.15 = bf16[1,2,32,16,128]{4,3,1,0,2:T(8,128)(2,1)S(1)} all-to-all(bf16[1,2,32,16,128]{4,3,1,0,2:T(8,128)(2,1)S(1)} %copy.40), channel_id=1, replica_groups=mesh['dp'=8,'shard'=32] {'shard'}, dimensions={2} | all-to-all | bytes 524288 | tf_op jit(solution)/shard_map/all_to_all | solution.py:42
  152.1 0.4 stack.3
  152.5 31.1 %all_to_all.16 = bf16[8,1,2,512,128]{4,3,2,1,0:T(8,128)(2,1)S(1)} all-to-all(bf16[8,1,2,512,128]{4,3,2,1,0:T(8,128)(2,1)S(1)} %stack.3), channel_id=1, replica_groups=mesh['dp'=8,'shard'=32] {'dp'}, dimensions={0} | all-to-all | bytes 4194304 | tf_op jit(solution)/shard_map/all_to_all | solution.py:9
  183.5 1.5 copy.42
  (2 shorter events, 0.1 us)
Async XLA Ops:
  7.2 97.3 %reduce-scatter.2.cloned.1.call-start = ((), (), s32[]{:S(2)}) async-start(), calls=%async_computation.4 | async-start | bytes 4718592 | tf_op jit(solution)/shard_map/reduce_scatter | solution.py:25
  7.9 109.2 %copy-start.3 = (f32[64]{0:T(128)S(1)}, f32[64]{0:T(128)}, u32[]{:S(2)}) copy-start(f32[64]{0:T(128)} %param.12) | copy-start | bytes 772
  7.9 124.7 %copy-start = (f32[1,2,16,4096]{3,2,1,0:T(8,128)S(1)}, f32[1,2,16,4096]{3,2,1,0:T(8,128)}, u32[]{:S(2)}) copy-start(f32[1,2,16,4096]{3,2,1,0:T(8,128)} %param.8) | copy-start | bytes 1572868
  7.9 124.7 %copy-start.1 = (f32[1,2,16,4096]{3,2,1,0:T(8,128)S(1)}, f32[1,2,16,4096]{3,2,1,0:T(8,128)}, u32[]{:S(2)}) copy-start(f32[1,2,16,4096]{3,2,1,0:T(8,128)} %param.10) | copy-start | bytes 1572868
  7.9 124.7 %copy-start.2 = (f32[1,2,16,4096]{3,2,1,0:T(8,128)S(1)}, f32[1,2,16,4096]{3,2,1,0:T(8,128)}, u32[]{:S(2)}) copy-start(f32[1,2,16,4096]{3,2,1,0:T(8,128)} %param.9) | copy-start | bytes 1572868
  106.4 25.9 %all-to-all-start = ((f32[1,2,32,16,128]{4,3,1,0,2:T(8,128)}), f32[1,2,32,16,128]{4,3,1,0,2:T(8,128)S(1)}, u32[]{:S(2)}, u32[]{:S(2)}) async-start(f32[1,2,32,16,128]{4,3,1,0,2:T(8,128)} %copy.34), calls=%async_computation.1 | async-start | bytes 1048576 | tf_op jit(solution)/shard_map/all_to_all | solution.py:27
Sparse Core Ops, SparseCore 0:
  12.1 92.3 reduce-scatter.1
